TPU v7x, 512 devices: a whole 4x8x8 slice. The times are simulated.
512 devices in a mesh: table: 64 (over y, z), expert: 8 (over x, core).
Axes of the slice: x: 4, y: 8, z: 8, core: 2. Of those that a mesh axis runs over, the one named last changes fastest.
Arguments:
- table: bfloat16 [64, 512, 256], P('table'), may hold values from -127 to 127, as said below
- row_scale: float32 [64, 512], P('table'), may hold values from 0.3 to 3
- windows: int32 [64, 8, 256], P('table', 'expert'), may hold values from 0 to 511, as said below
- bag_idx: int32 [64, 8, 8192, 8], P('table', 'expert'), may hold values from 0 to 255
- bag_len: int32 [64, 8, 8192], P('table', 'expert'), may hold values from 1 to 8
- feat_gain: float32 [64, 256], replicated, may hold values from 0.03 to 0.3
- norm_gain: float32 [256], replicated, may hold values from 0.5 to 1.5
- expert_ids: int32 [8, 8192, 1], P('expert', 'table'), may hold values from 0 to 63; in each aligned block of 128 rows (0 to 127, 128 to 255, ..., all dimensions but the last counted through in order) at most 4 rows name the same one
- w_in: bfloat16 [64, 256, 4096], P('table', None, 'expert'), may hold values from -0.375 to 0.375
- w_out: bfloat16 [64, 4096, 256], P('table', 'expert'), may hold values from -0.09375 to 0.09375
- w_tow1: bfloat16 [3, 256, 256], replicated, may hold values from -0.375 to 0.375
- w_tow2: float32 [3, 256], replicated, may hold values from -1.5 to 1.5
- targets: float32 [8, 8192, 3], P('expert', 'table'), may hold values from 0 to 1
Outputs:
- predictions: float32 [8, 8192, 3], P('expert', 'table')
- grad_table: float32 [64, 512, 256], P('table', 'expert')
- grad_w_in: float32 [64, 256, 4096], P('table', None, 'expert')
- grad_w_out: float32 [64, 4096, 256], P('table', 'expert')
Inputs may be any that keep to these rules, and one draw needn't show every extreme that they name: `table`: every entry is an integer. Each row windows[f, g] holds 256 distinct row numbers of feature f's table. `expert_ids`: in each aligned block of 128 samples (the samples of one device) no expert is named by more than 4 samples.
All inputs are finite; a program needn't handle non-finite values.
Results may differ from a plain program's by a relative error of at most 0.02.
Values may be sent and summed in bfloat16 or wider, within the bound.
No kernel may reach another device: no remote copies, remote signals or barrier semaphores. Data moves between devices by JAX's collectives and lax.ppermute only.
A program may use at most 128 MiB of HBM per device.

v0:
```python
import math
import jax
import jax.numpy as jnp
from jax import lax
from jax.sharding import PartitionSpec as P

code_range = 127.0


def silu_slope(values):
    sigma = jax.nn.sigmoid(values)
    return sigma * (1.0 + values * (1.0 - sigma))


def bag_counts(indices, lengths, window):
    total = indices.shape[0]
    block = math.gcd(total, 512)
    positions = jnp.arange(window, dtype=jnp.int32)
    slots = jnp.arange(indices.shape[1], dtype=jnp.int32)

    def count_block(operands):
        block_idx, block_len = operands
        live = (slots[None, :] < block_len[:, None]).astype(jnp.float32)
        hits = (block_idx[:, :, None] == positions[None, None, :]).astype(jnp.float32)
        return jnp.sum(hits * live[:, :, None], axis=1).astype(jnp.bfloat16)

    blocked = lax.map(
        count_block,
        (
            indices.reshape(total // block, block, indices.shape[1]),
            lengths.reshape(total // block, block),
        ),
    )
    return blocked.reshape(total, window)


def dispatch(buffer):
    arrived = lax.all_to_all(buffer, "table", split_axis=0, concat_axis=0, tiled=True)
    columns = lax.all_gather(arrived[None], "expert", axis=0, tiled=True)
    return columns.reshape(-1, buffer.shape[-1])


def column_sum(term_fn, local_rows):
    return lax.psum_scatter(
        term_fn(jnp.int32(0), lax.axis_size("expert") * local_rows).astype(jnp.bfloat16),
        "expert",
        scatter_dimension=0,
        tiled=True,
    ).astype(jnp.float32)


def send_back(result, experts, capacity):
    rows_back = result.astype(jnp.bfloat16).reshape(experts, capacity, result.shape[-1])
    arrived = lax.all_to_all(rows_back, "table", split_axis=0, concat_axis=0, tiled=True)
    return arrived.reshape(experts * capacity, result.shape[-1])


def local(
    table,
    row_scale,
    windows,
    bag_idx,
    bag_len,
    feat_gain,
    norm_gain,
    expert_ids,
    w_in,
    w_out,
    w_tow1,
    w_tow2,
    targets,
):
    owners = lax.axis_size("table")
    samples = expert_ids.shape[1]
    capacity = max(2, 2 * samples // owners)
    local_rows = owners * capacity
    contract_rows = (((0,), (0,)), ((), ()))
    contract_cols = (((1,), (1,)), ((), ()))
    window = windows[0, 0]
    picked = jnp.take(table[0], window, axis=0).astype(jnp.float32)
    scales = jnp.take(row_scale[0], window)
    dequant = (picked * scales[:, None] / code_range).astype(jnp.bfloat16)
    counts = bag_counts(bag_idx[0, 0], bag_len[0, 0], window.shape[0])
    pooled = jnp.dot(counts, dequant, preferred_element_type=jnp.float32).astype(jnp.bfloat16)
    features = lax.all_to_all(
        pooled.reshape(owners, samples, pooled.shape[-1]),
        "table",
        split_axis=0,
        concat_axis=0,
        tiled=True,
    )
    summed = jnp.sum(features.astype(jnp.float32) * feat_gain[:, None, :], axis=0)
    inverse = lax.rsqrt(jnp.mean(summed * summed, axis=-1, keepdims=True) + 1e-05)
    normed = (summed * inverse * norm_gain).astype(jnp.bfloat16)
    chosen = expert_ids[0, :, 0]
    member = (chosen[:, None] == jnp.arange(owners, dtype=jnp.int32)[None, :]).astype(jnp.int32)
    ranks = jnp.cumsum(member, axis=0) - member
    slot_of = jnp.sum(ranks * member, axis=1)
    target_slot = chosen * capacity + slot_of
    placing = (jnp.arange(local_rows, dtype=jnp.int32)[:, None] == target_slot[None, :]).astype(
        jnp.bfloat16
    )
    outgoing = jnp.dot(placing, normed, preferred_element_type=jnp.float32).astype(jnp.bfloat16)
    gathered = dispatch(outgoing.reshape(owners, capacity, outgoing.shape[-1]))
    weight_in = w_in[0]
    weight_out = w_out[0]
    pre_act = jnp.dot(gathered, weight_in, preferred_element_type=jnp.float32)
    hidden = jax.nn.silu(pre_act).astype(jnp.bfloat16)

    def forward_term(start, count):
        return jnp.dot(hidden, weight_out, preferred_element_type=jnp.float32)

    expert_out = send_back(column_sum(forward_term, local_rows), owners, capacity)
    mixture = lax.dot_general(
        placing, expert_out, contract_rows, preferred_element_type=jnp.float32
    )
    joined = (normed.astype(jnp.float32) + mixture).astype(jnp.bfloat16)
    tower_pre = jnp.einsum("be,kem->kbm", joined, w_tow1, preferred_element_type=jnp.float32)
    logits = jnp.sum(jax.nn.silu(tower_pre) * w_tow2[:, None, :], axis=-1)
    predicted = jnp.stack(
        [jax.nn.sigmoid(logits[0]), jax.nn.sigmoid(logits[1]), logits[2]], axis=-1
    )
    logit_grad = predicted - targets[0]
    tower_grad = (logit_grad.T[:, :, None] * w_tow2[:, None, :] * silu_slope(tower_pre)).astype(
        jnp.bfloat16
    )
    joined_grad = jnp.einsum(
        "kbm,kem->be", tower_grad, w_tow1, preferred_element_type=jnp.float32
    ).astype(jnp.bfloat16)
    back_rows = jnp.dot(placing, joined_grad, preferred_element_type=jnp.float32).astype(
        jnp.bfloat16
    )
    gathered_grad = dispatch(back_rows.reshape(owners, capacity, back_rows.shape[-1]))
    grad_hidden = lax.dot_general(
        gathered_grad, weight_out, contract_cols, preferred_element_type=jnp.float32
    )
    grad_pre = (grad_hidden * silu_slope(pre_act)).astype(jnp.bfloat16)
    grad_out = lax.dot_general(
        hidden, gathered_grad, contract_rows, preferred_element_type=jnp.float32
    )
    grad_in = lax.dot_general(gathered, grad_pre, contract_rows, preferred_element_type=jnp.float32)

    def backward_term(start, count):
        return lax.dot_general(
            grad_pre, weight_in, contract_cols, preferred_element_type=jnp.float32
        )

    input_grad = send_back(column_sum(backward_term, local_rows), owners, capacity)
    mixture_grad = lax.dot_general(
        placing, input_grad, contract_rows, preferred_element_type=jnp.float32
    )
    normed_grad = joined_grad.astype(jnp.float32) + mixture_grad
    scaled_grad = normed_grad * norm_gain
    summed_grad = inverse * (
        scaled_grad
        - summed * inverse * inverse * jnp.mean(scaled_grad * summed, axis=-1, keepdims=True)
    )
    feature_grad = (summed_grad[None, :, :] * feat_gain[:, None, :]).astype(jnp.bfloat16)
    returned = lax.all_to_all(
        feature_grad, "table", split_axis=0, concat_axis=0, tiled=True
    ).reshape(owners * samples, feature_grad.shape[-1])
    window_grad = lax.dot_general(
        counts, returned, contract_rows, preferred_element_type=jnp.float32
    )
    row_select = (jnp.arange(table.shape[1], dtype=jnp.int32)[:, None] == window[None, :]).astype(
        jnp.float32
    )
    row_grad = jnp.dot(row_select, window_grad, precision=lax.Precision.HIGHEST)
    table_grad = lax.psum_scatter(
        row_grad.astype(jnp.bfloat16), "expert", scatter_dimension=0, tiled=True
    ).astype(jnp.float32)
    return (predicted[None], table_grad[None], grad_in[None], grad_out[None])


def solution(mesh):
    in_specs = (
        P("table", None, None),
        P("table", None),
        P("table", "expert", None),
        P("table", "expert", None, None),
        P("table", "expert", None),
        P(),
        P(),
        P("expert", "table", None),
        P("table", None, "expert"),
        P("table", "expert", None),
        P(),
        P(),
        P("expert", "table", None),
    )
    out_specs = (
        P("expert", "table", None),
        P("table", "expert", None),
        P("table", None, "expert"),
        P("table", "expert", None),
    )
    return jax.shard_map(local, mesh=mesh, in_specs=in_specs, out_specs=out_specs, check_vma=False)
```

profile of v0, /device:TPU:8, one launch (start us, length us, event | category | flops | bytes accessed | tf_op | source)
XLA Modules:
  0.0 661.4 jit_solution(6694098426931538434)
XLA Ops:
  8.4 1.5 reduce.3
  10.0 75.1 %while.11 = (s32[]{:T(128)}, bf16[16,512,256]{2,1,0:T(8,128)(2,1)}, s32[16,512,8]{1,2,0:T(8,128)}, s32[16,512]{1,0:T(8,128)S(1)}, s32[]{:T(128)}) while((s32[]{:T(128)}, bf16[16,512,256]{2,1,0:T(8,128)(2,1)}, s32[16,512,8]{1,2,0:T(8,128)}, s32[16,512]{1,0:T(8,128)S(1)}, s32[]{:T(128)}) %tuple.50), condition=%wide.region_2.3_spmd.clone, body=%wide.region_0.0_spmd.clone.sunk | while | flops 3022850 | bytes 940613 | solution.py:27
  11.0 3.0 select_reduce_fusion.3
  15.7 3.0 select_reduce_fusion.3
  20.4 3.0 select_reduce_fusion.3
  25.1 3.0 select_reduce_fusion.3
  29.8 3.0 select_reduce_fusion.3
  34.5 3.0 select_reduce_fusion.3
  39.2 3.0 select_reduce_fusion.3
  43.9 3.0 select_reduce_fusion.3
  48.5 3.0 select_reduce_fusion.3
  53.2 3.0 select_reduce_fusion.3
  57.9 3.0 select_reduce_fusion.3
  62.6 3.0 select_reduce_fusion.3
  67.3 3.0 select_reduce_fusion.3
  72.0 3.0 select_reduce_fusion.3
  76.6 3.0 select_reduce_fusion.3
  81.3 3.0 select_reduce_fusion.3
  85.1 1.9 gather_fusion.1
  87.0 1.2 gather_fusion
  88.2 5.5 convolution_convert_fusion
  93.7 16.9 %all-to-all-start = ((bf16[64,128,256]{2,1,0:T(8,128)(2,1)}), bf16[64,128,256]{2,1,0:T(8,128)(2,1)}, u32[]{:S(2)}, u32[]{:S(2)}) async-start(bf16[64,128,256]{2,1,0:T(8,128)(2,1)} %bitcast.88), calls=%async_computation | async-start | bytes 8388608 | tf_op jit(solution)/shard_map/all_to_all | solution.py:85
  111.2 126.4 %all-to-all-done = bf16[64,128,256]{2,1,0:T(8,128)(2,1)} async-done(((bf16[64,128,256]{2,1,0:T(8,128)(2,1)}), bf16[64,128,256]{2,1,0:T(8,128)(2,1)}, u32[]{:S(2)}, u32[]{:S(2)}) %all-to-all-start) | async-done | bytes 4194336 | tf_op jit(solution)/shard_map/all_to_all | solution.py:85
  237.6 3.1 multiply_reduce_fusion
  241.1 27.0 %all_to_all.30 = bf16[64,4,256]{2,1,0:T(4,128)(2,1)} all-to-all(bf16[64,4,256]{2,1,0:T(4,128)(2,1)S(1)} %reshape.210), channel_id=1, replica_groups=mesh['table'=64,'expert'=8] {'table'}, dimensions={0} | all-to-all | bytes 262144 | tf_op jit(solution)/shard_map/all_to_all | solution.py:38
  268.2 20.6 %all-gather.5.cloned.1.call-done = bf16[512,4,256]{2,1,0:T(4,128)(2,1)} async-done(((bf16[64,4,256]{2,1,0:T(4,128)(2,1)}), bf16[512,4,256]{2,1,0:T(4,128)(2,1)}) %all-gather.5.cloned.1.call-update) | async-done | bytes 1048592 | tf_op jit(solution)/shard_map/all_gather | solution.py:39
  288.8 1.3 reshape.211
  290.2 3.1 multiply_convert_fusion.2
  293.3 1.3 copy-done.3
  294.7 1.7 convolution_convert_fusion.2
  296.4 37.5 %reduce-scatter.4.cloned.1.call-done = bf16[256,256]{1,0:T(8,128)(2,1)} async-done(((bf16[2048,256]{1,0:T(8,128)(2,1)}), bf16[256,256]{1,0:T(8,128)(2,1)}) %reduce-scatter.4.cloned.1.call-update) | async-done | bytes 131088 | tf_op jit(solution)/shard_map/reduce_scatter | solution.py:44
  334.9 24.9 %all_to_all.31 = bf16[64,4,256]{2,1,0:T(4,128)(2,1)S(1)} all-to-all(bf16[64,4,256]{2,1,0:T(4,128)(2,1)S(1)} %reshape.212), channel_id=1, replica_groups=mesh['table'=64,'expert'=8] {'table'}, dimensions={0} | all-to-all | bytes 262144 | tf_op jit(solution)/shard_map/all_to_all | solution.py:54
  361.0 17.1 %all_to_all.32 = bf16[64,4,256]{2,1,0:T(4,128)(2,1)} all-to-all(bf16[64,4,256]{2,1,0:T(4,128)(2,1)S(1)} %reshape.214), channel_id=1, replica_groups=mesh['table'=64,'expert'=8] {'table'}, dimensions={0} | all-to-all | bytes 262144 | tf_op jit(solution)/shard_map/all_to_all | solution.py:38
  378.3 18.9 %all-gather.7.cloned.1.call-done = bf16[512,4,256]{2,1,0:T(4,128)(2,1)} async-done(((bf16[64,4,256]{2,1,0:T(4,128)(2,1)}), bf16[512,4,256]{2,1,0:T(4,128)(2,1)}) %all-gather.7.cloned.1.call-update) | async-done | bytes 1048592 | tf_op jit(solution)/shard_map/all_gather | solution.py:39
  397.3 1.3 reshape.215
  398.6 5.2 multiply_convert_fusion.1
  403.8 3.3 convolution_convert_fusion.1
  407.2 37.6 %reduce-scatter.6.cloned.1.call-done = bf16[256,256]{1,0:T(8,128)(2,1)} async-done(((bf16[2048,256]{1,0:T(8,128)(2,1)}), bf16[256,256]{1,0:T(8,128)(2,1)}) %reduce-scatter.6.cloned.1.call-update) | async-done | bytes 131088 | tf_op jit(solution)/shard_map/reduce_scatter | solution.py:44
  445.7 25.0 %all_to_all.33 = bf16[64,4,256]{2,1,0:T(4,128)(2,1)S(1)} all-to-all(bf16[64,4,256]{2,1,0:T(4,128)(2,1)S(1)} %reshape.216), channel_id=1, replica_groups=mesh['table'=64,'expert'=8] {'table'}, dimensions={0} | all-to-all | bytes 262144 | tf_op jit(solution)/shard_map/all_to_all | solution.py:54
  471.2 3.4 multiply_convert_fusion
  474.6 6.4 all-to-all-start.5
  481.7 105.1 %all-to-all-done.5 = bf16[64,128,256]{2,1,0:T(8,128)(2,1)} async-done(((bf16[64,128,256]{2,1,0:T(8,128)(2,1)}), bf16[64,128,256]{2,1,0:T(8,128)(2,1)}, u32[]{:S(2)}, u32[]{:S(2)}) %all-to-all-start.5) | async-done | bytes 4194336 | tf_op jit(solution)/shard_map/all_to_all | solution.py:159
  586.8 4.7 fusion.35
  591.5 1.1 convolution_convert_fusion.3
  592.7 3.4 convolution_bitcast_fusion.1
  596.1 1.5 convolution_bitcast_fusion
  597.6 55.8 %reduce-scatter.8.cloned.1.call-done = bf16[64,256]{1,0:T(8,128)(2,1)} async-done(((bf16[512,256]{1,0:T(8,128)(2,1)}), bf16[64,256]{1,0:T(8,128)(2,1)}) %reduce-scatter.8.cloned.1.call-update) | async-done | bytes 32784 | tf_op jit(solution)/shard_map/reduce_scatter | solution.py:169
  653.4 1.4 bitcast_convert_fusion
  (161 shorter events, 34.0 us)
Async XLA Ops:
  7.2 352.7 %copy-start = (bf16[3,256,256]{2,1,0:T(8,128)(2,1)S(1)}, bf16[3,256,256]{2,1,0:T(8,128)(2,1)}, u32[]{:S(2)}) copy-start(bf16[3,256,256]{2,1,0:T(8,128)(2,1)} %param.25) | copy-start | bytes 1179652
  9.9 75.1 %copy-start.1 = (f32[1,512]{1,0:T(1,128)S(1)}, f32[1,512]{1,0:T(1,128)}, u32[]{:S(2)}) copy-start(f32[1,512]{1,0:T(1,128)} %param.16) | copy-start | bytes 6148
  9.9 77.1 %copy-start.2 = (bf16[1,512,256]{2,1,0:T(8,128)(2,1)S(1)}, bf16[1,512,256]{2,1,0:T(8,128)(2,1)}, u32[]{:S(2)}) copy-start(bf16[1,512,256]{2,1,0:T(8,128)(2,1)} %param.15) | copy-start | bytes 786436
  10.0 78.2 %copy-start.8 = (s32[1,1,256]{2,1,0:T(1,128)S(1)}, s32[1,1,256]{2,1,0:T(1,128)}, u32[]{:S(2)}) copy-start(s32[1,1,256]{2,1,0:T(1,128)} %param.17) | copy-start | bytes 3076
  93.7 17.0 %copy-start.10 = (s32[1,128,1]{1,2,0:T(1,128)S(1)}, s32[1,128,1]{1,2,0:T(1,128)}, u32[]{:S(2)}) copy-start(s32[1,128,1]{1,2,0:T(1,128)} %param.22) | copy-start | bytes 1540
  93.7 143.9 %copy-start.6 = (f32[64,256]{1,0:T(8,128)S(1)}, f32[64,256]{1,0:T(8,128)}, u32[]{:S(2)}) copy-start(f32[64,256]{1,0:T(8,128)} %param.20) | copy-start | bytes 196612
  93.7 143.9 %all-to-all-start = ((bf16[64,128,256]{2,1,0:T(8,128)(2,1)}), bf16[64,128,256]{2,1,0:T(8,128)(2,1)}, u32[]{:S(2)}, u32[]{:S(2)}) async-start(bf16[64,128,256]{2,1,0:T(8,128)(2,1)} %bitcast.88), calls=%async_computation | async-start | bytes 8388608 | tf_op jit(solution)/shard_map/all_to_all | solution.py:85
  110.6 130.2 %copy-start.9 = (f32[256]{0:T(256)S(1)}, f32[256]{0:T(256)}, u32[]{:S(2)}) copy-start(f32[256]{0:T(256)} %param.21) | copy-start | bytes 3076
  110.6 179.5 %copy-start.7 = (bf16[1,256,512]{2,1,0:T(8,128)(2,1)S(1)}, bf16[1,256,512]{2,1,0:T(8,128)(2,1)}, u32[]{:S(2)}) copy-start(bf16[1,256,512]{2,1,0:T(8,128)(2,1)} %param.23) | copy-start | bytes 786436
  110.7 178.2 %all-gather.5.cloned.1.call-start = ((), (), s32[]{:S(2)}) async-start(), calls=%async_computation.12 | async-start | bytes 1179648 | tf_op jit(solution)/shard_map/all_gather | solution.py:39
  268.1 65.9 %reduce-scatter.4.cloned.1.call-start = ((), (), s32[]{:S(2)}) async-start(), calls=%async_computation.9 | async-start | bytes 1179648 | tf_op jit(solution)/shard_map/reduce_scatter | solution.py:44
  290.2 3.2 copy-start.5
  290.2 4.5 copy-start.12
  293.3 1.3 copy-start.3
  293.3 66.5 %copy-start.13 = (f32[3,256]{1,0:T(4,128)S(1)}, f32[3,256]{1,0:T(4,128)}, u32[]{:S(2)}) copy-start(f32[3,256]{1,0:T(4,128)} %param.26) | copy-start | bytes 9220
  294.7 65.8 %copy-start.11 = (f32[1,128,3]{1,0,2:T(1,128)S(1)}, f32[1,128,3]{1,0,2:T(1,128)}, u32[]{:S(2)}) copy-start(f32[1,128,3]{1,0,2:T(1,128)} %param.27) | copy-start | bytes 4612
  296.4 100.9 %all-gather.7.cloned.1.call-start = ((), (), s32[]{:S(2)}) async-start(), calls=%async_computation.13 | async-start | bytes 1179648 | tf_op jit(solution)/shard_map/all_gather | solution.py:39
  378.1 66.6 %reduce-scatter.6.cloned.1.call-start = ((), (), s32[]{:S(2)}) async-start(), calls=%async_computation.10 | async-start | bytes 1179648 | tf_op jit(solution)/shard_map/reduce_scatter | solution.py:44
  474.6 112.1 %all-to-all-start.5 = ((bf16[64,128,256]{2,1,0:T(8,128)(2,1)}), bf16[64,128,256]{2,1,0:T(8,128)(2,1)}, u32[]{:S(2)}, u32[]{:S(2)}) async-start(bf16[64,128,256]{2,1,0:T(8,128)(2,1)} %multiply_convert_fusion), calls=%async_computation.7 | async-start | bytes 8388608 | tf_op jit(solution)/shard_map/all_to_all | solution.py:159
  481.0 172.4 %reduce-scatter.8.cloned.1.call-start = ((), (), s32[]{:S(2)}) async-start(), calls=%async_computation.11 | async-start | bytes 294912 | tf_op jit(solution)/shard_map/reduce_scatter | solution.py:169
  591.5 4.6 copy-start.4
Sparse Core Ops, SparseCore 0:
  268.2 20.5 all-gather.4
  296.5 37.4 reduce-scatter.3
  378.2 18.9 all-gather.6
  407.3 37.4 reduce-scatter.5
  592.8 60.6 reduce-scatter.7
where the time goes:
time: 663 us; the launch traced here: 661 us
  waiting for transfers between devices  402 us (61%)
  blocking collectives  94 us (14%)
  other arithmetic  58.2 us (9%)
  local copies, waits for them, and re-layouts  37.5 us (6%)
  matrix products  31.3 us (5%)
  starting transfers between devices  23.7 us (4%)
  between operations  14.1 us (2%)
    all_to_all x1, waiting for transfers between devices, local(): lax.all_to_all(pooled.reshape(owners, samples, pooled.shape[-1]), 'table'...  126 us
    all_to_all x1, waiting for transfers between devices, local(): lax.all_to_all(feature_grad, 'table', split_axis=0, concat_axis=0, tiled=...  105 us
    reduce_scatter x2, waiting for transfers between devices, column_sum(): lax.psum_scatter(term_fn(jnp.int32(0), lax.axis_size('expert') * local_ro...  75.1 us
    reduce_scatter x1, waiting for transfers between devices, local(): lax.psum_scatter(row_grad.astype(jnp.bfloat16), 'expert', scatter_dimensi...  55.8 us
    all_to_all x2, blocking collectives, send_back(): lax.all_to_all(rows_back, 'table', split_axis=0, concat_axis=0, tiled=True)  49.9 us
    reduce_sum x16, other arithmetic, count_block(): return jnp.sum(hits * live[:, :, None], axis=1).astype(jnp.bfloat16)  47.3 us
    all_to_all x2, blocking collectives, dispatch(): lax.all_to_all(buffer, 'table', split_axis=0, concat_axis=0, tiled=True)  44 us
    all_gather x2, waiting for transfers between devices, dispatch(): columns = lax.all_gather(arrived[None], 'expert', axis=0, tiled=True)  39.6 us
  transfers between devices with their start and end apart: 7, of which 7 were waited for; matrix products, arithmetic and copies ran while one was open for 1% of the time, Pallas kernels for 0%

commit v1 on v0

--- a/solution.py
+++ b/solution.py
@@ -5,6 +5,24 @@
 from jax.sharding import PartitionSpec as P
 
 code_range = 127.0
+
+
+def ring_gather(shard, axis, dim):
+    ways, here, step = (lax.axis_size(axis), lax.axis_index(axis), shard.shape[dim])
+    lengths = [n * ways if d == dim else n for d, n in enumerate(shard.shape)]
+    full = lax.dynamic_update_slice_in_dim(
+        jnp.zeros(lengths, shard.dtype), shard, here * step, axis=dim
+    )
+    going_up = going_down = shard
+    for far in range(1, ways // 2 + 1):
+        going_up = lax.ppermute(going_up, axis, [(d, (d + 1) % ways) for d in range(ways)])
+        full = lax.dynamic_update_slice_in_dim(full, going_up, (here - far) % ways * step, axis=dim)
+        if 2 * far < ways:
+            going_down = lax.ppermute(going_down, axis, [(d, (d - 1) % ways) for d in range(ways)])
+            full = lax.dynamic_update_slice_in_dim(
+                full, going_down, (here + far) % ways * step, axis=dim
+            )
+    return full
 
 
 def silu_slope(values):
@@ -36,7 +54,7 @@
 
 def dispatch(buffer):
     arrived = lax.all_to_all(buffer, "table", split_axis=0, concat_axis=0, tiled=True)
-    columns = lax.all_gather(arrived[None], "expert", axis=0, tiled=True)
+    columns = ring_gather(arrived[None], "expert", 0)
     return columns.reshape(-1, buffer.shape[-1])
 
 

time: 663 us -> 644 us (0.971)
  starting transfers between devices: 23.7 us -> 68.4 us
  waiting for transfers between devices: 402 us -> 365 us
  blocking collectives: 94 us -> 66.5 us
    all_gather x2 -> x0, waiting for transfers between devices: 39.6 us -> none  [dispatch(): columns = lax.all_gather(arrived[None], 'expert', axis=0, tiled=True)]
    all_to_all x2 -> x1, blocking collectives: 44 us -> 16.8 us  [dispatch(): lax.all_to_all(buffer, 'table', split_axis=0, concat_axis=0, tiled=True)]
    all_to_all x0 -> x1, starting transfers between devices: none -> 27.2 us  [dispatch(): lax.all_to_all(buffer, 'table', split_axis=0, concat_axis=0, tiled=True)]
    ppermute x0 -> x14, waiting for transfers between devices: none -> 25.5 us  [the longest x8 25.5 us: ring_gather(): lax.ppermute(going_up, axis, [(d, (d + 1) % ways) for d in range(ways)])]
    reduce_scatter x2, waiting for transfers between devices: 75.1 us -> 55 us  [column_sum(): lax.psum_scatter(term_fn(jnp.int32(0), lax.axis_size('expert') * local_ro...]
    ppermute x0 -> x14, starting transfers between devices: none -> 17.8 us  [the longest x6 17.7 us: ring_gather(): lax.ppermute(going_down, axis, [(d, (d - 1) % ways) for d in range(ways)])]
    all_to_all x0 -> x1, waiting for transfers between devices: none -> 11.7 us  [dispatch(): lax.all_to_all(buffer, 'table', split_axis=0, concat_axis=0, tiled=True)]
    reduce_scatter x1, waiting for transfers between devices: 55.8 us -> 44.8 us  [local(): lax.psum_scatter(row_grad.astype(jnp.bfloat16), 'expert', scatter_dimensi...]
  transfers between devices with their start and end apart: 7 -> 20, of which waited for: 7 -> 14; matrix products, arithmetic and copies ran while one was open for 1% -> 1% of each run, Pallas kernels for 0% -> 0%
where the time goes in v1:
time: 644 us; the launch traced here: 642 us
  waiting for transfers between devices  365 us (57%)
  starting transfers between devices  68.4 us (11%)
  blocking collectives  66.5 us (10%)
  other arithmetic  58.2 us (9%)
  local copies, waits for them, and re-layouts  37.8 us (6%)
  matrix products  31.3 us (5%)
  between operations  14.3 us (2%)
    all_to_all x1, waiting for transfers between devices, local(): lax.all_to_all(pooled.reshape(owners, samples, pooled.shape[-1]), 'table'...  118 us
    all_to_all x1, waiting for transfers between devices, local(): lax.all_to_all(feature_grad, 'table', split_axis=0, concat_axis=0, tiled=...  110 us
    reduce_scatter x2, waiting for transfers between devices, column_sum(): lax.psum_scatter(term_fn(jnp.int32(0), lax.axis_size('expert') * local_ro...  55 us
    all_to_all x2, blocking collectives, send_back(): lax.all_to_all(rows_back, 'table', split_axis=0, concat_axis=0, tiled=True)  49.8 us
    reduce_sum x16, other arithmetic, count_block(): return jnp.sum(hits * live[:, :, None], axis=1).astype(jnp.bfloat16)  47.3 us
    reduce_scatter x1, waiting for transfers between devices, local(): lax.psum_scatter(row_grad.astype(jnp.bfloat16), 'expert', scatter_dimensi...  44.8 us
    all_to_all x1, starting transfers between devices, dispatch(): lax.all_to_all(buffer, 'table', split_axis=0, concat_axis=0, tiled=True)  27.2 us
    ppermute x8, waiting for transfers between devices, ring_gather(): lax.ppermute(going_up, axis, [(d, (d + 1) % ways) for d in range(ways)])  25.5 us
  transfers between devices with their start and end apart: 20, of which 14 were waited for; matrix products, arithmetic and copies ran while one was open for 1% of the time, Pallas kernels for 0%

profile of v1, /device:TPU:8, one launch (start us, length us, event | category | flops | bytes accessed | tf_op | source)
XLA Modules:
  0.0 642.0 jit_solution(2391561098147133246)
XLA Ops:
  10.0 75.2 %while.11 = (s32[]{:T(128)}, bf16[16,512,256]{2,1,0:T(8,128)(2,1)}, s32[16,512,8]{1,2,0:T(8,128)}, s32[16,512]{1,0:T(8,128)S(1)}, s32[]{:T(128)}) while((s32[]{:T(128)}, bf16[16,512,256]{2,1,0:T(8,128)(2,1)}, s32[16,512,8]{1,2,0:T(8,128)}, s32[16,512]{1,0:T(8,128)S(1)}, s32[]{:T(128)}) %tuple.45), condition=%wide.region_2.3_spmd.clone, body=%wide.region_0.0_spmd.clone.sunk | while | flops 3022850 | bytes 940613 | solution.py:45
  11.0 3.0 select_reduce_fusion.3
  15.7 3.0 select_reduce_fusion.3
  20.4 3.0 select_reduce_fusion.3
  25.1 3.0 select_reduce_fusion.3
  29.8 3.0 select_reduce_fusion.3
  34.5 3.0 select_reduce_fusion.3
  39.2 3.0 select_reduce_fusion.3
  43.9 3.0 select_reduce_fusion.3
  48.6 3.0 select_reduce_fusion.3
  53.3 3.0 select_reduce_fusion.3
  58.0 3.0 select_reduce_fusion.3
  62.7 3.0 select_reduce_fusion.3
  67.4 3.0 select_reduce_fusion.3
  72.1 3.0 select_reduce_fusion.3
  76.8 3.0 select_reduce_fusion.3
  81.5 3.0 select_reduce_fusion.3
  88.3 5.5 convolution_convert_fusion
  93.8 16.9 %all-to-all-start = ((bf16[64,128,256]{2,1,0:T(8,128)(2,1)}), bf16[64,128,256]{2,1,0:T(8,128)(2,1)}, u32[]{:S(2)}, u32[]{:S(2)}) async-start(bf16[64,128,256]{2,1,0:T(8,128)(2,1)} %bitcast.92), calls=%async_computation | async-start | bytes 8388608 | tf_op jit(solution)/shard_map/all_to_all | solution.py:103
  111.2 118.3 %all-to-all-done = bf16[64,128,256]{2,1,0:T(8,128)(2,1)} async-done(((bf16[64,128,256]{2,1,0:T(8,128)(2,1)}), bf16[64,128,256]{2,1,0:T(8,128)(2,1)}, u32[]{:S(2)}, u32[]{:S(2)}) %all-to-all-start) | async-done | bytes 4194336 | tf_op jit(solution)/shard_map/all_to_all | solution.py:103
  229.5 3.1 multiply_reduce_fusion
  233.7 27.2 %all-to-all-start.1 = ((bf16[64,4,256]{2,1,0:T(4,128)(2,1)}), bf16[64,4,256]{2,1,0:T(4,128)(2,1)S(1)}, u32[]{:S(2)}, u32[]{:S(2)}) async-start(bf16[64,4,256]{2,1,0:T(4,128)(2,1)} %reshape.210), calls=%async_computation.1 | async-start | bytes 262144 | tf_op jit(solution)/shard_map/all_to_all | solution.py:56
  261.1 11.7 %all-to-all-done.1 = bf16[64,4,256]{2,1,0:T(4,128)(2,1)S(1)} async-done(((bf16[64,4,256]{2,1,0:T(4,128)(2,1)}), bf16[64,4,256]{2,1,0:T(4,128)(2,1)S(1)}, u32[]{:S(2)}, u32[]{:S(2)}) %all-to-all-start.1) | async-done | bytes 131104 | tf_op jit(solution)/shard_map/all_to_all | solution.py:56
  272.7 3.0 collective-permute-start.1
  278.3 3.0 collective-permute-start.3
  281.4 2.5 collective-permute-done.2
  283.9 3.0 collective-permute-start.5
  287.0 2.5 collective-permute-done.4
  289.7 5.5 collective-permute-done.6
  295.5 3.2 multiply_convert_fusion.2
  301.8 27.5 %reduce-scatter.4.cloned.1.call-done = bf16[256,256]{1,0:T(8,128)(2,1)} async-done(((bf16[2048,256]{1,0:T(8,128)(2,1)}), bf16[256,256]{1,0:T(8,128)(2,1)}) %reduce-scatter.4.cloned.1.call-update) | async-done | bytes 131088 | tf_op jit(solution)/shard_map/reduce_scatter | solution.py:62
  330.2 24.9 %all_to_all.30 = bf16[64,4,256]{2,1,0:T(4,128)(2,1)S(1)} all-to-all(bf16[64,4,256]{2,1,0:T(4,128)(2,1)S(1)} %reshape.212), channel_id=1, replica_groups=mesh['table'=64,'expert'=8] {'table'}, dimensions={0} | all-to-all | bytes 262144 | tf_op jit(solution)/shard_map/all_to_all | solution.py:72
  356.3 16.8 %all_to_all.31 = bf16[64,4,256]{2,1,0:T(4,128)(2,1)S(1)} all-to-all(bf16[64,4,256]{2,1,0:T(4,128)(2,1)S(1)} %reshape.214), channel_id=1, replica_groups=mesh['table'=64,'expert'=8] {'table'}, dimensions={0} | all-to-all | bytes 262144 | tf_op jit(solution)/shard_map/all_to_all | solution.py:56
  373.1 3.0 collective-permute-start.8
  378.8 3.0 collective-permute-start.10
  381.8 2.5 collective-permute-done.9
  384.4 3.0 collective-permute-start.12
  390.1 5.4 collective-permute-done.13
  395.9 5.2 multiply_convert_fusion.1
  401.1 3.3 convolution_convert_fusion.1
  404.4 27.5 %reduce-scatter.6.cloned.1.call-done = bf16[256,256]{1,0:T(8,128)(2,1)} async-done(((bf16[2048,256]{1,0:T(8,128)(2,1)}), bf16[256,256]{1,0:T(8,128)(2,1)}) %reduce-scatter.6.cloned.1.call-update) | async-done | bytes 131088 | tf_op jit(solution)/shard_map/reduce_scatter | solution.py:62
  432.9 24.8 %all_to_all.32 = bf16[64,4,256]{2,1,0:T(4,128)(2,1)S(1)} all-to-all(bf16[64,4,256]{2,1,0:T(4,128)(2,1)S(1)} %reshape.216), channel_id=1, replica_groups=mesh['table'=64,'expert'=8] {'table'}, dimensions={0} | all-to-all | bytes 262144 | tf_op jit(solution)/shard_map/all_to_all | solution.py:72
  458.2 3.4 multiply_convert_fusion
  461.6 6.4 %all-to-all-start.5 = ((bf16[64,128,256]{2,1,0:T(8,128)(2,1)}), bf16[64,128,256]{2,1,0:T(8,128)(2,1)}, u32[]{:S(2)}, u32[]{:S(2)}) async-start(bf16[64,128,256]{2,1,0:T(8,128)(2,1)} %multiply_convert_fusion), calls=%async_computation.7 | async-start | bytes 8388608 | tf_op jit(solution)/shard_map/all_to_all | solution.py:177
  468.7 109.8 %all-to-all-done.5 = bf16[64,128,256]{2,1,0:T(8,128)(2,1)} async-done(((bf16[64,128,256]{2,1,0:T(8,128)(2,1)}), bf16[64,128,256]{2,1,0:T(8,128)(2,1)}, u32[]{:S(2)}, u32[]{:S(2)}) %all-to-all-start.5) | async-done | bytes 4194336 | tf_op jit(solution)/shard_map/all_to_all | solution.py:177
  578.5 4.7 fusion.35
  584.4 3.4 convolution_bitcast_fusion.1
  589.3 44.8 %reduce-scatter.8.cloned.1.call-done = bf16[64,256]{1,0:T(8,128)(2,1)} async-done(((bf16[512,256]{1,0:T(8,128)(2,1)}), bf16[64,256]{1,0:T(8,128)(2,1)}) %reduce-scatter.8.cloned.1.call-update) | async-done | bytes 32784 | tf_op jit(solution)/shard_map/reduce_scatter | solution.py:187
  (202 shorter events, 55.4 us)
Async XLA Ops:
  7.2 348.0 %copy-start = (bf16[3,256,256]{2,1,0:T(8,128)(2,1)S(1)}, bf16[3,256,256]{2,1,0:T(8,128)(2,1)}, u32[]{:S(2)}) copy-start(bf16[3,256,256]{2,1,0:T(8,128)(2,1)} %param.25) | copy-start | bytes 1179652
  9.9 75.2 %copy-start.1 = (f32[1,512]{1,0:T(1,128)S(1)}, f32[1,512]{1,0:T(1,128)}, u32[]{:S(2)}) copy-start(f32[1,512]{1,0:T(1,128)} %param.16) | copy-start | bytes 6148
  9.9 77.2 %copy-start.2 = (bf16[1,512,256]{2,1,0:T(8,128)(2,1)S(1)}, bf16[1,512,256]{2,1,0:T(8,128)(2,1)}, u32[]{:S(2)}) copy-start(bf16[1,512,256]{2,1,0:T(8,128)(2,1)} %param.15) | copy-start | bytes 786436
  10.0 78.3 %copy-start.8 = (s32[1,1,256]{2,1,0:T(1,128)S(1)}, s32[1,1,256]{2,1,0:T(1,128)}, u32[]{:S(2)}) copy-start(s32[1,1,256]{2,1,0:T(1,128)} %param.17) | copy-start | bytes 3076
  93.8 16.9 %copy-start.10 = (s32[1,128,1]{1,2,0:T(1,128)S(1)}, s32[1,128,1]{1,2,0:T(1,128)}, u32[]{:S(2)}) copy-start(s32[1,128,1]{1,2,0:T(1,128)} %param.22) | copy-start | bytes 1540
  93.8 135.7 %copy-start.6 = (f32[64,256]{1,0:T(8,128)S(1)}, f32[64,256]{1,0:T(8,128)}, u32[]{:S(2)}) copy-start(f32[64,256]{1,0:T(8,128)} %param.20) | copy-start | bytes 196612
  93.8 135.7 %all-to-all-start = ((bf16[64,128,256]{2,1,0:T(8,128)(2,1)}), bf16[64,128,256]{2,1,0:T(8,128)(2,1)}, u32[]{:S(2)}, u32[]{:S(2)}) async-start(bf16[64,128,256]{2,1,0:T(8,128)(2,1)} %bitcast.92), calls=%async_computation | async-start | bytes 8388608 | tf_op jit(solution)/shard_map/all_to_all | solution.py:103
  110.8 122.0 %copy-start.9 = (f32[256]{0:T(256)S(1)}, f32[256]{0:T(256)}, u32[]{:S(2)}) copy-start(f32[256]{0:T(256)} %param.21) | copy-start | bytes 3076
  232.6 62.9 %copy-start.7 = (bf16[1,256,512]{2,1,0:T(8,128)(2,1)S(1)}, bf16[1,256,512]{2,1,0:T(8,128)(2,1)}, u32[]{:S(2)}) copy-start(bf16[1,256,512]{2,1,0:T(8,128)(2,1)} %param.23) | copy-start | bytes 786436
  233.7 39.0 %all-to-all-start.1 = ((bf16[64,4,256]{2,1,0:T(4,128)(2,1)}), bf16[64,4,256]{2,1,0:T(4,128)(2,1)S(1)}, u32[]{:S(2)}, u32[]{:S(2)}) async-start(bf16[64,4,256]{2,1,0:T(4,128)(2,1)} %reshape.210), calls=%async_computation.1 | async-start | bytes 262144 | tf_op jit(solution)/shard_map/all_to_all | solution.py:56
  260.9 68.4 %reduce-scatter.4.cloned.1.call-start = ((), (), s32[]{:S(2)}) async-start(), calls=%async_computation.9 | async-start | bytes 1179648 | tf_op jit(solution)/shard_map/reduce_scatter | solution.py:62
  272.7 5.6 collective-permute-start
  272.7 5.6 collective-permute-start.1
  278.3 5.6 collective-permute-start.2
  278.3 5.6 collective-permute-start.3
  283.9 5.6 collective-permute-start.4
  283.9 5.7 collective-permute-start.5
  289.5 5.6 collective-permute-start.6
  295.5 3.2 copy-start.5
  295.5 4.5 copy-start.12
  298.7 1.3 copy-start.3
  298.7 56.5 %copy-start.13 = (f32[3,256]{1,0:T(4,128)S(1)}, f32[3,256]{1,0:T(4,128)}, u32[]{:S(2)}) copy-start(f32[3,256]{1,0:T(4,128)} %param.26) | copy-start | bytes 9220
  300.1 55.7 %copy-start.11 = (f32[1,128,3]{1,0,2:T(1,128)S(1)}, f32[1,128,3]{1,0,2:T(1,128)}, u32[]{:S(2)}) copy-start(f32[1,128,3]{1,0,2:T(1,128)} %param.27) | copy-start | bytes 4612
  301.8 130.2 %reduce-scatter.6.cloned.1.call-start = ((), (), s32[]{:S(2)}) async-start(), calls=%async_computation.10 | async-start | bytes 1179648 | tf_op jit(solution)/shard_map/reduce_scatter | solution.py:62
  373.1 5.6 collective-permute-start.7
  373.1 5.7 collective-permute-start.8
  378.7 5.6 collective-permute-start.9
  378.8 5.6 collective-permute-start.10
  384.3 5.6 collective-permute-start.11
  384.4 5.6 collective-permute-start.12
  389.9 5.6 collective-permute-start.13
  461.6 116.8 %all-to-all-start.5 = ((bf16[64,128,256]{2,1,0:T(8,128)(2,1)}), bf16[64,128,256]{2,1,0:T(8,128)(2,1)}, u32[]{:S(2)}, u32[]{:S(2)}) async-start(bf16[64,128,256]{2,1,0:T(8,128)(2,1)} %multiply_convert_fusion), calls=%async_computation.7 | async-start | bytes 8388608 | tf_op jit(solution)/shard_map/all_to_all | solution.py:177
  468.1 166.0 %reduce-scatter.8.cloned.1.call-start = ((), (), s32[]{:S(2)}) async-start(), calls=%async_computation.11 | async-start | bytes 294912 | tf_op jit(solution)/shard_map/reduce_scatter | solution.py:187
  583.2 4.6 copy-start.4
Sparse Core Ops, SparseCore 0:
  301.9 27.3 reduce-scatter.3
  404.6 27.3 reduce-scatter.5
  584.5 49.5 reduce-scatter.7
